TPU v7x, 256 devices: a whole 4x4x8 slice. The times are simulated.
256 devices in a mesh: det: 16 (over z, core), orb: 16 (over x, y).
Axes of the slice: x: 4, y: 4, z: 8, core: 2. Of those that a mesh axis runs over, the one named last changes fastest.
Arguments:
- orbitals: bfloat16 [64, 1024, 256], P('det', 'orb'), may hold values from -0.06 to 1.06
- dfit: bfloat16 [64, 1024, 1024], P('orb'), may hold values from -0.5 to 0.5, as said below
- pair_left: int32 [32], P('det'), may hold values from 0 to 63, as said below
- pair_right: int32 [32], P('det'), may hold values from 0 to 63
- pair_count: int32 [16], P('det'), may hold values from 1 to 2, as said below
- pair_weight: float32 [32], P('det'), may hold values from 1 to 4
- aux_screen: int32 [32, 64], P('det', 'orb'), may hold values 0 or 1
Outputs:
- gradient: float32 [64, 1024, 256], P('det', 'orb')
Inputs may be any that keep to these rules, and one draw needn't show every extreme that they name: `pair_left`: slot s names a determinant among numbers (s // 2) * 4 to (s // 2 + 1) * 4 - 1. `pair_count`: some det index has all 2 slots live. `dfit`: every matrix is symmetric.
All inputs are finite; a program needn't handle non-finite values. No bound on the sum of `aux_screen` on one device may be relied on, other than what follows from the above.
Results may differ from a plain program's by a relative error of at most 0.0022.
Values may be sent and summed in bfloat16 or wider, within the bound.
No kernel may reach another device: no remote copies, remote signals or barrier semaphores. Data moves between devices by JAX's collectives and lax.ppermute only.
A program may use at most 64 MiB of HBM per device.

v0:
```python
import jax
import jax.numpy as jnp
from jax import lax
from jax.sharding import PartitionSpec as P

NS = 3


def newton(correlation):
    eye = jnp.eye(correlation.shape[-1], dtype=jnp.float32)
    inverse = jnp.broadcast_to(eye, correlation.shape)
    for sweep in range(NS):
        product = jnp.einsum("bij,bjk->bik", correlation, inverse, precision=lax.Precision.HIGHEST)
        inverse = jnp.einsum(
            "bij,bjk->bik", inverse, 2.0 * eye - product, precision=lax.Precision.HIGHEST
        )
    return inverse


def process(dfit, left_rows, right_rows, weights, screen):
    correlation_part = jnp.einsum(
        "brc,brd->bcd", left_rows, right_rows, preferred_element_type=jnp.float32
    )
    correlation = lax.psum(correlation_part, "orb")
    inverse = newton(correlation)
    moved_rows = jnp.einsum(
        "brc,bcd->brd", right_rows.astype(jnp.float32), inverse, precision=lax.Precision.HIGHEST
    ).astype(jnp.bfloat16)
    left_full, moved_full = (
        lax.all_gather(left_rows, "orb", axis=1, tiled=True),
        lax.all_gather(moved_rows, "orb", axis=1, tiled=True),
    )
    applied = jnp.einsum(
        "qst,btc->bqsc", dfit, moved_full, preferred_element_type=jnp.float32
    ).astype(jnp.bfloat16)
    projected = jnp.einsum(
        "bsc,qst->bqct", left_full, dfit, preferred_element_type=jnp.float32
    ).astype(jnp.bfloat16)
    exchange = jnp.einsum(
        "bqct,btd->bqcd", projected, moved_full, preferred_element_type=jnp.float32
    )
    factor = 2.0 * weights[:, None, None, None] * screen.astype(jnp.float32)[:, :, None, None]
    scaled = (factor * exchange).astype(jnp.bfloat16)
    left_term = jnp.einsum("bqsc,bqdc->sbd", applied, scaled, preferred_element_type=jnp.float32)
    moved_term = jnp.einsum("bqcs,bqcd->sbd", projected, scaled, preferred_element_type=jnp.float32)
    summed = lax.psum_scatter(
        jnp.concatenate([left_term, moved_term], axis=1), "orb", scatter_dimension=0, tiled=True
    )
    batch = left_rows.shape[0]
    left_grad = jnp.transpose(summed[:, :batch], (1, 0, 2))
    moved_grad = jnp.transpose(summed[:, batch:], (1, 0, 2))
    right_grad = jnp.einsum("brc,bdc->brd", moved_grad, inverse, precision=lax.Precision.HIGHEST)
    return (left_grad, right_grad)


def local(orbitals, dfit, pair_left, pair_right, pair_count, pair_weight, aux_screen):
    det_local = orbitals.shape[0]
    capacity = pair_left.shape[0]
    slot_index = jnp.arange(capacity, dtype=jnp.int32)
    weights = jnp.where(slot_index < pair_count[0], pair_weight, jnp.zeros_like(pair_weight))
    left_local = pair_left % det_local
    left_rows = jnp.take(orbitals, left_local, axis=0)
    everyone = lax.all_gather(orbitals, "det", axis=0, tiled=True)
    right_rows = jnp.take(everyone, pair_right, axis=0)

    def one_slot(slot, grads):

        def select_slot(array):
            return lax.dynamic_slice_in_dim(array, slot, 1, 0)

        left_one, right_one = process(
            dfit,
            select_slot(left_rows),
            select_slot(right_rows),
            select_slot(weights),
            select_slot(aux_screen),
        )
        return (
            lax.dynamic_update_slice_in_dim(grads[0], left_one, slot, 0),
            lax.dynamic_update_slice_in_dim(grads[1], right_one, slot, 0),
        )

    zeros = jnp.zeros(left_rows.shape, jnp.float32)
    left_grad, right_grad = lax.fori_loop(0, capacity, one_slot, (zeros, zeros))
    owners = (left_local[:, None] == jnp.arange(det_local, dtype=jnp.int32)[None, :]).astype(
        jnp.float32
    )
    own_sum = jnp.einsum("pn,prc->nrc", owners, left_grad, precision=lax.Precision.HIGHEST)
    places = jnp.arange(det_local * lax.axis_size("det"), dtype=jnp.int32)
    match = (pair_right[:, None] == places[None, :]).astype(jnp.float32)
    returned = lax.psum_scatter(
        jnp.einsum("pn,prc->nrc", match, right_grad, precision=lax.Precision.HIGHEST),
        "det",
        scatter_dimension=0,
        tiled=True,
    )
    return own_sum + returned


def solution(mesh):
    in_specs = (
        P("det", "orb", None),
        P("orb", None, None),
        P("det"),
        P("det"),
        P("det"),
        P("det"),
        P("det", "orb"),
    )
    out_specs = P("det", "orb", None)
    return jax.shard_map(local, mesh=mesh, in_specs=in_specs, out_specs=out_specs, check_vma=False)
```

profile of v0, /device:TPU:4, one launch (start us, length us, event | category | flops | bytes accessed | tf_op | source)
XLA Modules:
  0.0 620.7 jit_solution(5396601231880543745)
XLA Ops:
  8.6 1.5 gather_fusion
  12.1 39.4 %all-gather.5.cloned.1.call-done = bf16[64,64,256]{2,1,0:T(8,128)(2,1)} async-done(((bf16[4,64,256]{2,1,0:T(8,128)(2,1)}), bf16[64,64,256]{2,1,0:T(8,128)(2,1)}) %all-gather.5.cloned.1.call-update) | async-done | bytes 2097168 | tf_op jit(solution)/shard_map/all_gather | solution.py:63
  51.6 2.1 gather_fusion.1
  53.8 486.6 %while.15 = (s32[]{:T(128)}, f32[2,64,256]{2,0,1:T(2,128)}, f32[2,64,256]{2,0,1:T(2,128)}, f32[2]{0:T(128)S(1)}, s32[2,4]{1,0:T(2,128)}, /*index=5*/bf16[2,64,25...) while((s32[]{:T(128)}, f32[2,64,256]{2,0,1:T(2,128)}, ...), condition=%wide.region_3.4_spmd, body=%wide.region_0.3_spmd.sunk | while | flops 7227064320 | bytes 65279744 | solution.py:84
  54.9 23.7 %all_gather.19 = bf16[1,1024,256]{2,1,0:T(8,128)(2,1)S(1)} all-gather(bf16[1,64,256]{2,1,0:T(8,128)(2,1)S(1)} %constant_dynamic-slice_fusion.6), channel_id=1, replica_groups=mesh['det'=16,'orb'=16] {'orb'}, dimensions={1}, use_global_device_ids=true | all-gather | bytes 557056 | tf_op jit(solution)/shard_map/while/body/eval_jaxpr/all_gather | solution.py:30
  78.5 5.8 convolution_convert_fusion.4
  85.6 64.8 %all-reduce.6.cloned.1.call-done = f32[256,256]{1,0:T(8,128)} async-done(((f32[256,256]{1,0:T(8,128)}), f32[256,256]{1,0:T(8,128)}) %all-reduce.6.cloned.1.call-update) | async-done | bytes 262160 | tf_op jit(solution)/shard_map/while/body/eval_jaxpr/psum | solution.py:24
  154.7 22.7 %all-gather.2 = bf16[1024,256]{1,0:T(8,128)(2,1)S(1)} all-gather(bf16[64,256]{1,0:T(8,128)(2,1)S(1)} %convolution_convert_fusion.5), channel_id=2, replica_groups=mesh['det'=16,'orb'=16] {'orb'}, dimensions={0}, use_global_device_ids=true | all-gather | bytes 557056 | tf_op jit(solution)/shard_map/while/body/eval_jaxpr/all_gather | solution.py:31
  180.5 7.7 %fusion.137 = f32[1024,1,256]{0,2,1:T(8,128)} fusion(bf16[4,256,256]{2,1,0:T(8,128)(2,1)} %copy-done.1, bf16[4,1024,1024]{2,1,0:T(8,128)(2,1)} %get-tuple-element.280, bf16[1024,256]{1,0:T(8,128)(2,1)} %copy-done.2), kind=kOutput, calls=%fused_computation.12.clone.1 | convolution fusion | flops 2685403136 | bytes 10485760 | tf_op jit(solution)/shard_map/while/body/eval_jaxpr/bqsc,bqdc->sbd/dot_general | solution.py:44
  188.2 1.4 pad_maximum_fusion.2
  189.6 2.4 copy.46
  193.8 98.1 %all-reduce.8.cloned.1.call-done = f32[1024,2,256]{2,1,0:T(2,128)} async-done(((f32[1024,2,256]{2,1,0:T(2,128)}), f32[1024,2,256]{2,1,0:T(2,128)}) %all-reduce.8.cloned.1.call-update) | async-done | bytes 2097168 | tf_op jit(solution)/shard_map/while
  297.0 23.4 %all_gather.19 = bf16[1,1024,256]{2,1,0:T(8,128)(2,1)S(1)} all-gather(bf16[1,64,256]{2,1,0:T(8,128)(2,1)S(1)} %constant_dynamic-slice_fusion.6), channel_id=1, replica_groups=mesh['det'=16,'orb'=16] {'orb'}, dimensions={1}, use_global_device_ids=true | all-gather | bytes 557056 | tf_op jit(solution)/shard_map/while/body/eval_jaxpr/all_gather | solution.py:30
  320.4 5.8 convolution_convert_fusion.4
  327.4 67.3 %all-reduce.6.cloned.1.call-done = f32[256,256]{1,0:T(8,128)} async-done(((f32[256,256]{1,0:T(8,128)}), f32[256,256]{1,0:T(8,128)}) %all-reduce.6.cloned.1.call-update) | async-done | bytes 262160 | tf_op jit(solution)/shard_map/while/body/eval_jaxpr/psum | solution.py:24
  399.1 22.7 %all-gather.2 = bf16[1024,256]{1,0:T(8,128)(2,1)S(1)} all-gather(bf16[64,256]{1,0:T(8,128)(2,1)S(1)} %convolution_convert_fusion.5), channel_id=2, replica_groups=mesh['det'=16,'orb'=16] {'orb'}, dimensions={0}, use_global_device_ids=true | all-gather | bytes 557056 | tf_op jit(solution)/shard_map/while/body/eval_jaxpr/all_gather | solution.py:31
  424.9 7.7 %fusion.137 = f32[1024,1,256]{0,2,1:T(8,128)} fusion(bf16[4,256,256]{2,1,0:T(8,128)(2,1)} %copy-done.1, bf16[4,1024,1024]{2,1,0:T(8,128)(2,1)} %get-tuple-element.280, bf16[1024,256]{1,0:T(8,128)(2,1)} %copy-done.2), kind=kOutput, calls=%fused_computation.12.clone.1 | convolution fusion | flops 2685403136 | bytes 10485760 | tf_op jit(solution)/shard_map/while/body/eval_jaxpr/bqsc,bqdc->sbd/dot_general | solution.py:44
  432.5 1.4 pad_maximum_fusion.2
  433.9 2.4 copy.46
  438.2 98.1 %all-reduce.8.cloned.1.call-done = f32[1024,2,256]{2,1,0:T(2,128)} async-done(((f32[1024,2,256]{2,1,0:T(2,128)}), f32[1024,2,256]{2,1,0:T(2,128)}) %all-reduce.8.cloned.1.call-update) | async-done | bytes 2097168 | tf_op jit(solution)/shard_map/while
  540.4 2.8 fusion.39
  543.2 4.4 copy.30
  549.0 63.2 %reduce-scatter.2.cloned.1.call-done = f32[4,64,256]{2,1,0:T(8,128)} async-done(((f32[64,64,256]{2,1,0:T(8,128)}), f32[4,64,256]{2,1,0:T(8,128)}) %reduce-scatter.2.cloned.1.call-update) | async-done | bytes 262160 | tf_op jit(solution)/shard_map/reduce_scatter | solution.py:91
  612.2 1.7 copy_add_fusion
  (102 shorter events, 33.4 us)
Async XLA Ops:
  6.5 45.0 %all-gather.5.cloned.1.call-start = ((), (), s32[]{:S(2)}) async-start(), calls=%async_computation.1 | async-start | bytes 2228224 | tf_op jit(solution)/shard_map/all_gather | solution.py:63
  53.8 486.6 %copy-start.9 = (s32[2]{0:T(128)S(1)}, s32[2]{0:T(128)}, u32[]{:S(2)}) copy-start(s32[2]{0:T(128)} %param.12) | copy-start | bytes 28
  53.8 96.5 %all-reduce.6.cloned.1.call-start = ((), (), s32[]{:S(2)}) async-start(), calls=%async_computation.3 | async-start | bytes 524288 | tf_op jit(solution)/shard_map/while/body/eval_jaxpr/psum | solution.py:24
  54.8 237.1 %all-reduce.8.cloned.1.call-start = ((), (), s32[]{:S(2)}) async-start(), calls=%async_computation.4 | async-start | bytes 4194304 | tf_op jit(solution)/shard_map/while
  78.5 7.0 %copy-start.8 = (s32[2,4]{1,0:T(2,128)S(1)}, s32[2,4]{1,0:T(2,128)}, u32[]{:S(2)}) copy-start(s32[2,4]{1,0:T(2,128)} %get-tuple-element.278) | copy-start | bytes 100 | tf_op jit(solution)/shard_map/while
  150.4 3.3 copy-start
  177.4 0.8 copy-start.2
  179.0 0.8 copy-start.1
  191.9 0.7 copy-start.10
  192.0 101.5 %copy-start.5 = (f32[2,64,256]{2,0,1:T(2,128)S(1)}, f32[2,64,256]{2,0,1:T(2,128)}, u32[]{:S(2)}) copy-start(f32[2,64,256]{2,0,1:T(2,128)} %get-tuple-element.260) | copy-start | bytes 393220 | tf_op jit(solution)/shard_map/while
  192.0 102.5 %copy-start.3 = (f32[2,64,256]{2,0,1:T(2,128)S(1)}, f32[2,64,256]{2,0,1:T(2,128)}, u32[]{:S(2)}) copy-start(f32[2,64,256]{2,0,1:T(2,128)} %get-tuple-element.261) | copy-start | bytes 393220 | tf_op jit(solution)/shard_map/while
  294.4 1.0 copy-start.6
  296.0 98.7 %all-reduce.6.cloned.1.call-start = ((), (), s32[]{:S(2)}) async-start(), calls=%async_computation.3 | async-start | bytes 524288 | tf_op jit(solution)/shard_map/while/body/eval_jaxpr/psum | solution.py:24
  296.9 239.4 %all-reduce.8.cloned.1.call-start = ((), (), s32[]{:S(2)}) async-start(), calls=%async_computation.4 | async-start | bytes 4194304 | tf_op jit(solution)/shard_map/while
  320.4 7.0 %copy-start.8 = (s32[2,4]{1,0:T(2,128)S(1)}, s32[2,4]{1,0:T(2,128)}, u32[]{:S(2)}) copy-start(s32[2,4]{1,0:T(2,128)} %get-tuple-element.278) | copy-start | bytes 100 | tf_op jit(solution)/shard_map/while
  394.7 3.3 copy-start
  421.8 0.8 copy-start.2
  423.3 0.8 copy-start.1
  436.3 0.7 copy-start.10
  436.3 101.5 %copy-start.5 = (f32[2,64,256]{2,0,1:T(2,128)S(1)}, f32[2,64,256]{2,0,1:T(2,128)}, u32[]{:S(2)}) copy-start(f32[2,64,256]{2,0,1:T(2,128)} %get-tuple-element.260) | copy-start | bytes 393220 | tf_op jit(solution)/shard_map/while
  436.3 102.5 %copy-start.3 = (f32[2,64,256]{2,0,1:T(2,128)S(1)}, f32[2,64,256]{2,0,1:T(2,128)}, u32[]{:S(2)}) copy-start(f32[2,64,256]{2,0,1:T(2,128)} %get-tuple-element.261) | copy-start | bytes 393220 | tf_op jit(solution)/shard_map/while
  538.8 1.0 copy-start.6
  540.4 71.8 %reduce-scatter.2.cloned.1.call-start = ((), (), s32[]{:S(2)}) async-start(), calls=%async_computation.2 | async-start | bytes 4456448 | tf_op jit(solution)/shard_map/reduce_scatter | solution.py:91
  547.6 0.9 copy-start.7
  (2 other events, 1.3 us)
Sparse Core Ops, SparseCore 0:
  9.2 42.3 all-gather.4
  57.8 92.5 all-reduce.5
  192.1 99.8 all-reduce.7
  299.7 94.9 all-reduce.5
  436.4 99.8 all-reduce.7
  547.7 64.3 reduce-scatter.1
where the time goes:
time: 621 us
  waiting for transfers between devices  432 us (70%)
  blocking collectives  92.5 us (15%)
  matrix products  44.2 us (7%)
  local copies, waits for them, and re-layouts  27.8 us (4%)
  between operations  14.1 us (2%)
  other arithmetic  7.37 us (1%)
    while x6, waiting for transfers between devices  196 us
    psum x2, waiting for transfers between devices, process(): correlation = lax.psum(correlation_part, 'orb')  132 us
    reduce_scatter x1, waiting for transfers between devices, local(): lax.psum_scatter(jnp.einsum('pn,prc->nrc', match, right_grad, precision=l...  63.2 us
    all_gather x2, blocking collectives, process(): lax.all_gather(left_rows, 'orb', axis=1, tiled=True)  47 us
    all_gather x2, blocking collectives, process(): lax.all_gather(moved_rows, 'orb', axis=1, tiled=True)  45.4 us
    all_gather x1, waiting for transfers between devices, local(): everyone = lax.all_gather(orbitals, 'det', axis=0, tiled=True)  39.4 us
    dot_general x2, matrix products, process(): jnp.einsum('bqsc,bqdc->sbd', applied, scaled, preferred_element_type=jnp....  15.3 us
  transfers between devices with their start and end apart: 6, of which 6 were waited for; matrix products, arithmetic and copies ran while one was open for 3% of the time, Pallas kernels for 0%

commit v1 on v0

--- a/solution.py
+++ b/solution.py
@@ -21,7 +21,13 @@
     correlation_part = jnp.einsum(
         "brc,brd->bcd", left_rows, right_rows, preferred_element_type=jnp.float32
     )
-    correlation = lax.psum(correlation_part, "orb")
+    size = lax.axis_size("orb")
+    correlation, far = (correlation_part, 1)
+    while far < size:
+        correlation = correlation + lax.ppermute(
+            correlation, "orb", [(i, i ^ far) for i in range(size)]
+        )
+        far = 2 * far
     inverse = newton(correlation)
     moved_rows = jnp.einsum(
         "brc,bcd->brd", right_rows.astype(jnp.float32), inverse, precision=lax.Precision.HIGHEST

time: 621 us -> 517 us (0.83)
  waiting for transfers between devices: 432 us -> 321 us
  starting transfers between devices: 0.14 us -> 15.4 us
    psum x2 -> x0, waiting for transfers between devices: 132 us -> none  [process(): correlation = lax.psum(correlation_part, 'orb')]
    ppermute x0 -> x8, waiting for transfers between devices: none -> 24 us  [process(): lax.ppermute(correlation, 'orb', [(i, i ^ far) for i in range(size)])]
    ppermute x0 -> x8, starting transfers between devices: none -> 15.4 us  [process(): lax.ppermute(correlation, 'orb', [(i, i ^ far) for i in range(size)])]
    while x6 -> x4, waiting for transfers between devices: 196 us -> 193 us
  transfers between devices with their start and end apart: 6 -> 12, of which waited for: 6 -> 8; matrix products, arithmetic and copies ran while one was open for 3% -> 4% of each run, Pallas kernels for 0% -> 0%
where the time goes in v1:
time: 517 us; the launch traced here: 516 us
  waiting for transfers between devices  321 us (62%)
  blocking collectives  91.7 us (18%)
  matrix products  38.2 us (7%)
  local copies, waits for them, and re-layouts  26.2 us (5%)
  starting transfers between devices  15.4 us (3%)
  between operations  13.8 us (3%)
  other arithmetic  7.58 us (1%)
    while x4, waiting for transfers between devices  193 us
    reduce_scatter x1, waiting for transfers between devices, local(): lax.psum_scatter(jnp.einsum('pn,prc->nrc', match, right_grad, precision=l...  63.2 us
    all_gather x2, blocking collectives, process(): lax.all_gather(left_rows, 'orb', axis=1, tiled=True)  46.3 us
    all_gather x2, blocking collectives, process(): lax.all_gather(moved_rows, 'orb', axis=1, tiled=True)  45.4 us
    all_gather x1, waiting for transfers between devices, local(): everyone = lax.all_gather(orbitals, 'det', axis=0, tiled=True)  39.4 us
    ppermute x8, waiting for transfers between devices, process(): lax.ppermute(correlation, 'orb', [(i, i ^ far) for i in range(size)])  24 us
    ppermute x8, starting transfers between devices, process(): lax.ppermute(correlation, 'orb', [(i, i ^ far) for i in range(size)])  15.4 us
    dot_general x2, matrix products, process(): jnp.einsum('bqsc,bqdc->sbd', applied, scaled, preferred_element_type=jnp....  14.6 us
  transfers between devices with their start and end apart: 12, of which 8 were waited for; matrix products, arithmetic and copies ran while one was open for 4% of the time, Pallas kernels for 0%

profile of v1, /device:TPU:4, one launch (start us, length us, event | category | flops | bytes accessed | tf_op | source)
XLA Modules:
  0.0 516.4 jit_solution(10603821030258585320)
XLA Ops:
  12.1 39.4 %all-gather.5.cloned.1.call-done = bf16[64,64,256]{2,1,0:T(8,128)(2,1)} async-done(((bf16[4,64,256]{2,1,0:T(8,128)(2,1)}), bf16[64,64,256]{2,1,0:T(8,128)(2,1)}) %all-gather.5.cloned.1.call-update) | async-done | bytes 2097168 | tf_op jit(solution)/shard_map/all_gather | solution.py:69
  53.8 382.5 %while.15 = (s32[]{:T(128)}, f32[2,64,256]{2,0,1:T(2,128)}, f32[2,64,256]{2,0,1:T(2,128)}, f32[2]{0:T(128)S(1)}, s32[2,4]{1,0:T(2,128)}, /*index=5*/bf16[2,64,25...) while((s32[]{:T(128)}, f32[2,64,256]{2,0,1:T(2,128)}, ...), condition=%wide.region_2.3_spmd, body=%wide.region_0.2_spmd.sunk | while | flops 7227392000 | bytes 64755436 | solution.py:90
  55.6 6.9 %collective-permute-done = f32[1,256,256]{2,1,0:T(8,128)S(1)} collective-permute-done((f32[1,256,256]{2,1,0:T(8,128)S(1)}, f32[1,256,256]{2,1,0:T(8,128)S(1)}, u32[]{:S(2)}, u32[]{:S(2)}) %collective-permute-start) | collective-permute-done | bytes 262176 | tf_op jit(solution)/shard_map/while/body/eval_jaxpr/ppermute | solution.py:27
  62.6 3.1 collective-permute-start.1
  65.7 6.1 %collective-permute-done.1 = f32[1,256,256]{2,1,0:T(8,128)S(1)} collective-permute-done((f32[1,256,256]{2,1,0:T(8,128)S(1)}, f32[1,256,256]{2,1,0:T(8,128)S(1)}, u32[]{:S(2)}, u32[]{:S(2)}) %collective-permute-start.1) | collective-permute-done | bytes 262176 | tf_op jit(solution)/shard_map/while/body/eval_jaxpr/ppermute | solution.py:27
  73.1 23.7 %all_gather.19 = bf16[1,1024,256]{2,1,0:T(8,128)(2,1)S(1)} all-gather(bf16[1,64,256]{2,1,0:T(8,128)(2,1)S(1)} %constant_dynamic-slice_fusion.6), channel_id=1, replica_groups=mesh['det'=16,'orb'=16] {'orb'}, dimensions={1}, use_global_device_ids=true | all-gather | bytes 557056 | tf_op jit(solution)/shard_map/while/body/eval_jaxpr/all_gather | solution.py:36
  98.4 5.8 %convolution_convert_fusion.4 = bf16[256,4,1024]{2,0,1:T(8,128)(2,1)S(1)} fusion(bf16[4,1024,1024]{2,1,0:T(8,128)(2,1)} %get-tuple-element.280, bf16[1,1024,256]{2,1,0:T(8,128)(2,1)S(1)} %all_gather.19), kind=kOutput, calls=%fused_computation.10.clone.1 | convolution fusion | flops 2148532224 | bytes 11010048 | tf_op jit(solution)/shard_map/while/body/eval_jaxpr/bsc,qst->bqct/dot_general | solution.py:42
  107.9 23.2 %all-gather.2 = bf16[1024,256]{1,0:T(8,128)(2,1)S(1)} all-gather(bf16[64,256]{1,0:T(8,128)(2,1)S(1)} %convolution_convert_fusion.5), channel_id=2, replica_groups=mesh['det'=16,'orb'=16] {'orb'}, dimensions={0}, use_global_device_ids=true | all-gather | bytes 557056 | tf_op jit(solution)/shard_map/while/body/eval_jaxpr/all_gather | solution.py:37
  132.5 7.3 %fusion.137 = f32[1024,1,256]{0,2,1:T(8,128)} fusion(bf16[4,256,256]{2,1,0:T(8,128)(2,1)S(1)} %fusion.135, bf16[4,1024,1024]{2,1,0:T(8,128)(2,1)} %get-tuple-element.280, bf16[1024,256]{1,0:T(8,128)(2,1)S(1)} %all-gather.2), kind=kOutput, calls=%fused_computation.12.clone.1 | convolution fusion | flops 2685403136 | bytes 10485760 | tf_op jit(solution)/shard_map/while/body/eval_jaxpr/bqsc,bqdc->sbd/dot_general | solution.py:50
  141.2 2.4 copy.46
  145.5 94.9 %all-reduce.5.cloned.1.call-done = f32[1024,2,256]{2,1,0:T(2,128)} async-done(((f32[1024,2,256]{2,1,0:T(2,128)}), f32[1024,2,256]{2,1,0:T(2,128)}) %all-reduce.5.cloned.1.call-update) | async-done | bytes 2097168 | tf_op jit(solution)/shard_map/while
  242.9 2.3 dynamic_update_slice.17
  246.7 5.5 %collective-permute-done = f32[1,256,256]{2,1,0:T(8,128)S(1)} collective-permute-done((f32[1,256,256]{2,1,0:T(8,128)S(1)}, f32[1,256,256]{2,1,0:T(8,128)S(1)}, u32[]{:S(2)}, u32[]{:S(2)}) %collective-permute-start) | collective-permute-done | bytes 262176 | tf_op jit(solution)/shard_map/while/body/eval_jaxpr/ppermute | solution.py:27
  252.2 2.5 collective-permute-start.1
  254.7 5.5 %collective-permute-done.1 = f32[1,256,256]{2,1,0:T(8,128)S(1)} collective-permute-done((f32[1,256,256]{2,1,0:T(8,128)S(1)}, f32[1,256,256]{2,1,0:T(8,128)S(1)}, u32[]{:S(2)}, u32[]{:S(2)}) %collective-permute-start.1) | collective-permute-done | bytes 262176 | tf_op jit(solution)/shard_map/while/body/eval_jaxpr/ppermute | solution.py:27
  262.3 22.5 %all_gather.19 = bf16[1,1024,256]{2,1,0:T(8,128)(2,1)S(1)} all-gather(bf16[1,64,256]{2,1,0:T(8,128)(2,1)S(1)} %constant_dynamic-slice_fusion.6), channel_id=1, replica_groups=mesh['det'=16,'orb'=16] {'orb'}, dimensions={1}, use_global_device_ids=true | all-gather | bytes 557056 | tf_op jit(solution)/shard_map/while/body/eval_jaxpr/all_gather | solution.py:36
  287.1 5.8 %convolution_convert_fusion.4 = bf16[256,4,1024]{2,0,1:T(8,128)(2,1)S(1)} fusion(bf16[4,1024,1024]{2,1,0:T(8,128)(2,1)} %get-tuple-element.280, bf16[1,1024,256]{2,1,0:T(8,128)(2,1)S(1)} %all_gather.19), kind=kOutput, calls=%fused_computation.10.clone.1 | convolution fusion | flops 2148532224 | bytes 11010048 | tf_op jit(solution)/shard_map/while/body/eval_jaxpr/bsc,qst->bqct/dot_general | solution.py:42
  296.5 22.3 %all-gather.2 = bf16[1024,256]{1,0:T(8,128)(2,1)S(1)} all-gather(bf16[64,256]{1,0:T(8,128)(2,1)S(1)} %convolution_convert_fusion.5), channel_id=2, replica_groups=mesh['det'=16,'orb'=16] {'orb'}, dimensions={0}, use_global_device_ids=true | all-gather | bytes 557056 | tf_op jit(solution)/shard_map/while/body/eval_jaxpr/all_gather | solution.py:37
  320.2 7.3 %fusion.137 = f32[1024,1,256]{0,2,1:T(8,128)} fusion(bf16[4,256,256]{2,1,0:T(8,128)(2,1)S(1)} %fusion.135, bf16[4,1024,1024]{2,1,0:T(8,128)(2,1)} %get-tuple-element.280, bf16[1024,256]{1,0:T(8,128)(2,1)S(1)} %all-gather.2), kind=kOutput, calls=%fused_computation.12.clone.1 | convolution fusion | flops 2685403136 | bytes 10485760 | tf_op jit(solution)/shard_map/while/body/eval_jaxpr/bqsc,bqdc->sbd/dot_general | solution.py:50
  328.9 2.4 copy.46
  333.2 98.3 %all-reduce.5.cloned.1.call-done = f32[1024,2,256]{2,1,0:T(2,128)} async-done(((f32[1024,2,256]{2,1,0:T(2,128)}), f32[1024,2,256]{2,1,0:T(2,128)}) %all-reduce.5.cloned.1.call-update) | async-done | bytes 2097168 | tf_op jit(solution)/shard_map/while
  436.3 2.8 fusion.44
  439.2 4.4 copy.30
  445.0 63.2 %reduce-scatter.2.cloned.1.call-done = f32[4,64,256]{2,1,0:T(8,128)} async-done(((f32[64,64,256]{2,1,0:T(8,128)}), f32[4,64,256]{2,1,0:T(8,128)}) %reduce-scatter.2.cloned.1.call-update) | async-done | bytes 262160 | tf_op jit(solution)/shard_map/reduce_scatter | solution.py:97
  (98 shorter events, 42.1 us)
Async XLA Ops:
  6.5 45.0 %all-gather.5.cloned.1.call-start = ((), (), s32[]{:S(2)}) async-start(), calls=%async_computation.1 | async-start | bytes 2228224 | tf_op jit(solution)/shard_map/all_gather | solution.py:69
  53.8 382.5 %copy-start.4 = (s32[2]{0:T(128)S(1)}, s32[2]{0:T(128)}, u32[]{:S(2)}) copy-start(s32[2]{0:T(128)} %param.12) | copy-start | bytes 28
  53.8 186.6 %all-reduce.5.cloned.1.call-start = ((), (), s32[]{:S(2)}) async-start(), calls=%async_computation.3 | async-start | bytes 4194304 | tf_op jit(solution)/shard_map/while
  54.1 8.5 %collective-permute-start = (f32[1,256,256]{2,1,0:T(8,128)S(1)}, f32[1,256,256]{2,1,0:T(8,128)S(1)}, u32[]{:S(2)}, u32[]{:S(2)}) collective-permute-start(f32[1,256,256]{2,1,0:T(8,128)S(1)} %convolution_bitcast_fusion.4), channel_id=1, source_target_pairs={{0,1},{1,0},{2,3},{3,2},{4,5},{5,4},{6,7},{7,6},{8,9},{9,8},{10,11... | collective-permute-start | bytes 786440 | tf_op jit(solution)/shard_map/while/body/eval_jaxpr/ppermute | solution.py:27
  62.6 9.2 %collective-permute-start.1 = (f32[1,256,256]{2,1,0:T(8,128)S(1)}, f32[1,256,256]{2,1,0:T(8,128)S(1)}, u32[]{:S(2)}, u32[]{:S(2)}) collective-permute-start(f32[1,256,256]{2,1,0:T(8,128)S(1)} %add.115), channel_id=1, source_target_pairs={{0,2},{1,3},{2,0},{3,1},{4,6},{5,7},{6,4},{7,5},{8,10},{9,11},{10,... | collective-permute-start | bytes 786440 | tf_op jit(solution)/shard_map/while/body/eval_jaxpr/ppermute | solution.py:27
  71.8 25.0 %collective-permute-start.2 = (f32[1,256,256]{2,1,0:T(8,128)S(1)}, f32[1,256,256]{2,1,0:T(8,128)S(1)}, u32[]{:S(2)}, u32[]{:S(2)}) collective-permute-start(f32[1,256,256]{2,1,0:T(8,128)S(1)} %add.116), channel_id=1, source_target_pairs={{0,4},{1,5},{2,6},{3,7},{4,0},{5,1},{6,2},{7,3},{8,12},{9,13},{10,... | collective-permute-start | bytes 786440 | tf_op jit(solution)/shard_map/while/body/eval_jaxpr/ppermute | solution.py:27
  96.9 8.6 %collective-permute-start.3 = (f32[1,256,256]{2,1,0:T(8,128)S(1)}, f32[1,256,256]{2,1,0:T(8,128)S(1)}, u32[]{:S(2)}, u32[]{:S(2)}) collective-permute-start(f32[1,256,256]{2,1,0:T(8,128)S(1)} %add.117), channel_id=1, source_target_pairs={{0,8},{1,9},{2,10},{3,11},{4,12},{5,13},{6,14},{7,15},{8,0},{9,1},... | collective-permute-start | bytes 786440 | tf_op jit(solution)/shard_map/while/body/eval_jaxpr/ppermute | solution.py:27
  98.4 7.0 %copy-start.3 = (s32[2,4]{1,0:T(2,128)S(1)}, s32[2,4]{1,0:T(2,128)}, u32[]{:S(2)}) copy-start(s32[2,4]{1,0:T(2,128)} %get-tuple-element.278) | copy-start | bytes 100 | tf_op jit(solution)/shard_map/while
  143.6 0.7 copy-start.5
  143.6 98.4 %copy-start = (f32[2,64,256]{2,0,1:T(2,128)S(1)}, f32[2,64,256]{2,0,1:T(2,128)}, u32[]{:S(2)}) copy-start(f32[2,64,256]{2,0,1:T(2,128)} %get-tuple-element.260) | copy-start | bytes 393220 | tf_op jit(solution)/shard_map/while
  242.9 2.3 copy-start.1
  245.3 186.2 %all-reduce.5.cloned.1.call-start = ((), (), s32[]{:S(2)}) async-start(), calls=%async_computation.3 | async-start | bytes 4194304 | tf_op jit(solution)/shard_map/while
  245.5 6.7 %collective-permute-start = (f32[1,256,256]{2,1,0:T(8,128)S(1)}, f32[1,256,256]{2,1,0:T(8,128)S(1)}, u32[]{:S(2)}, u32[]{:S(2)}) collective-permute-start(f32[1,256,256]{2,1,0:T(8,128)S(1)} %convolution_bitcast_fusion.4), channel_id=1, source_target_pairs={{0,1},{1,0},{2,3},{3,2},{4,5},{5,4},{6,7},{7,6},{8,9},{9,8},{10,11... | collective-permute-start | bytes 786440 | tf_op jit(solution)/shard_map/while/body/eval_jaxpr/ppermute | solution.py:27
  252.2 8.0 %collective-permute-start.1 = (f32[1,256,256]{2,1,0:T(8,128)S(1)}, f32[1,256,256]{2,1,0:T(8,128)S(1)}, u32[]{:S(2)}, u32[]{:S(2)}) collective-permute-start(f32[1,256,256]{2,1,0:T(8,128)S(1)} %add.115), channel_id=1, source_target_pairs={{0,2},{1,3},{2,0},{3,1},{4,6},{5,7},{6,4},{7,5},{8,10},{9,11},{10,... | collective-permute-start | bytes 786440 | tf_op jit(solution)/shard_map/while/body/eval_jaxpr/ppermute | solution.py:27
  260.2 24.6 %collective-permute-start.2 = (f32[1,256,256]{2,1,0:T(8,128)S(1)}, f32[1,256,256]{2,1,0:T(8,128)S(1)}, u32[]{:S(2)}, u32[]{:S(2)}) collective-permute-start(f32[1,256,256]{2,1,0:T(8,128)S(1)} %add.116), channel_id=1, source_target_pairs={{0,4},{1,5},{2,6},{3,7},{4,0},{5,1},{6,2},{7,3},{8,12},{9,13},{10,... | collective-permute-start | bytes 786440 | tf_op jit(solution)/shard_map/while/body/eval_jaxpr/ppermute | solution.py:27
  284.9 9.2 %collective-permute-start.3 = (f32[1,256,256]{2,1,0:T(8,128)S(1)}, f32[1,256,256]{2,1,0:T(8,128)S(1)}, u32[]{:S(2)}, u32[]{:S(2)}) collective-permute-start(f32[1,256,256]{2,1,0:T(8,128)S(1)} %add.117), channel_id=1, source_target_pairs={{0,8},{1,9},{2,10},{3,11},{4,12},{5,13},{6,14},{7,15},{8,0},{9,1},... | collective-permute-start | bytes 786440 | tf_op jit(solution)/shard_map/while/body/eval_jaxpr/ppermute | solution.py:27
  287.1 7.0 %copy-start.3 = (s32[2,4]{1,0:T(2,128)S(1)}, s32[2,4]{1,0:T(2,128)}, u32[]{:S(2)}) copy-start(s32[2,4]{1,0:T(2,128)} %get-tuple-element.278) | copy-start | bytes 100 | tf_op jit(solution)/shard_map/while
  331.3 0.7 copy-start.5
  331.3 101.7 %copy-start = (f32[2,64,256]{2,0,1:T(2,128)S(1)}, f32[2,64,256]{2,0,1:T(2,128)}, u32[]{:S(2)}) copy-start(f32[2,64,256]{2,0,1:T(2,128)} %get-tuple-element.260) | copy-start | bytes 393220 | tf_op jit(solution)/shard_map/while
  434.0 2.3 copy-start.1
  436.3 71.8 %reduce-scatter.2.cloned.1.call-start = ((), (), s32[]{:S(2)}) async-start(), calls=%async_computation.2 | async-start | bytes 4456448 | tf_op jit(solution)/shard_map/reduce_scatter | solution.py:97
  443.6 0.9 copy-start.2
Sparse Core Ops, SparseCore 0:
  9.2 42.3 all-gather.4
  143.8 96.6 all-reduce.4
  331.5 99.9 all-reduce.4
  443.7 64.3 reduce-scatter.1
